TPU v7x, 32 devices: a whole 2x2x4 slice. The times are simulated.
32 devices in a mesh: seq: 16 (over z, y, core), dp: 2 (over x).
Axes of the slice: x: 2, y: 2, z: 4, core: 2. Of those that a mesh axis runs over, the one named last changes fastest.
Arguments:
- queries: bfloat16 [2, 3072, 1536], P('dp', 'seq'), may hold values from -100 to 100
- key_vectors: bfloat16 [2, 3072, 1536], P('dp', 'seq'), may hold values from -6 to 6
- value_vectors: bfloat16 [2, 3072, 1536], P('dp', 'seq'), may hold values from -48 to 48
- w_out: bfloat16 [1536, 1536], P(('seq', 'dp')), may hold values from -0.15625 to 0.15625
- cotangent: bfloat16 [2, 3072, 1536], P('dp', 'seq'), may hold values from -0.119628906 to 0.119628906
Outputs:
- projected: bfloat16 [2, 3072, 1536], P('dp', 'seq')
- grad_w_out: float32 [1536, 1536], P(('seq', 'dp'))
All inputs are finite; a program needn't handle non-finite values.
Results may differ from a plain program's by a relative error of at most 0.0055.
Values may be sent and summed in bfloat16 or wider, within the bound.
No kernel may reach another device: no remote copies, remote signals or barrier semaphores. Data moves between devices by JAX's collectives and lax.ppermute only.
A program may use at most 128 MiB of HBM per device.

v0:
```python
import jax
import jax.numpy as jnp
from jax import lax
from jax.sharding import Mesh
from jax.sharding import PartitionSpec as P

HEADS = 8
HEAD_DIM = 192


def attend(query_here, key_all, value_all):
    query_count = query_here.shape[0]
    head_width = query_here.shape[1]
    block_size = min(512, query_count)
    score_scale = HEAD_DIM ** (-0.5)

    def one_block(query_block):
        scores = jnp.dot(query_block, key_all.T, preferred_element_type=jnp.float32) * score_scale
        largest = jnp.max(scores, axis=1, keepdims=True)
        raised = jnp.exp(scores - largest)
        denominator = jnp.sum(raised, axis=1, keepdims=True)
        weights = raised.astype(jnp.bfloat16)
        mixed = jnp.dot(weights, value_all, preferred_element_type=jnp.float32)
        return (mixed / denominator).astype(jnp.bfloat16)

    blocks = lax.map(
        one_block, query_here.reshape(query_count // block_size, block_size, head_width)
    )
    return blocks.reshape(query_count, head_width)


ALL = ("side", "inner", "dp")


def local(queries, key_vectors, value_vectors, w_out, cotangent):
    head_count = HEADS
    head_width = HEAD_DIM
    side_count = lax.axis_size("side")
    dp_count = lax.axis_size("dp")
    row_count = queries.shape[1]
    width = queries.shape[2]
    dp_index = lax.axis_index("dp")
    w_full = lax.all_gather(w_out, ALL, axis=0, tiled=True)
    cot_side = lax.all_gather(cotangent[0], "inner", axis=0, tiled=True)

    def a2a(tensor):
        return lax.all_to_all(tensor, "inner", split_axis=0, concat_axis=0, tiled=True)

    def by_head(tensor):
        return tensor[0].reshape(row_count, head_count, head_width).transpose(1, 0, 2)

    side_index = lax.axis_index("side")

    def by_lane(tensor):
        return tensor[0].reshape(row_count, head_count, head_width)

    kv_raw = jnp.concatenate([by_lane(key_vectors), by_lane(value_vectors)], axis=2)
    inner_index = lax.axis_index("inner")
    kv_crossed = []
    for step in range(1, side_count):
        for shift in range(head_count):
            perm = [
                (
                    g * head_count + i,
                    (g + step) % side_count * head_count + (i + shift) % head_count,
                )
                for g in range(side_count)
                for i in range(head_count)
            ]
            outgoing = lax.dynamic_index_in_dim(
                kv_raw, (inner_index + shift) % head_count, axis=1, keepdims=False
            )
            kv_crossed.append(lax.ppermute(outgoing, ("side", "inner"), perm))
    stacked = jnp.concatenate([by_lane(queries), kv_raw], axis=2)
    got = lax.all_to_all(stacked, "inner", split_axis=1, concat_axis=0, tiled=True).reshape(
        head_count * row_count, 3 * head_width
    )
    early = len(kv_crossed)
    kv_early, got = lax.optimization_barrier((kv_crossed[:early], got))
    kv_crossed = list(kv_early) + kv_crossed[early:]
    query_here = got[:, :head_width]
    kv_all = jnp.concatenate([got[:, head_width:]] + kv_crossed, axis=0)
    key_all = kv_all[:, :head_width]
    value_all = kv_all[:, head_width:]
    attended_here = attend(query_here, key_all, value_all)
    partial = lax.dot_general(
        attended_here, cot_side, (((0,), (0,)), ((), ())), preferred_element_type=jnp.float32
    )
    returned = a2a(attended_here.reshape(head_count, row_count, head_width))
    attended = returned.transpose(1, 0, 2).reshape(row_count, width)
    projected = jnp.dot(attended, w_full, preferred_element_type=jnp.float32).astype(jnp.bfloat16)
    chunk_count = side_count * dp_count
    chunk = head_width // chunk_count
    side_index = lax.axis_index("side")
    if dp_count == 2:
        pieces = partial.reshape(side_count, dp_count, chunk, width)
        kept = lax.dynamic_index_in_dim(pieces, dp_index, axis=1, keepdims=False)
        sent = lax.dynamic_index_in_dim(pieces, 1 - dp_index, axis=1, keepdims=False)
        kept = kept + lax.ppermute(sent, "dp", [(0, 1), (1, 0)])
        grad_w_out = None
        for step in range(side_count):
            perm = []
            for g in range(side_count):
                for h in range(head_count):
                    for p in range(dp_count):
                        owner_side = (g + step) % side_count
                        source = (g * head_count + h) * dp_count + p
                        target = (side_count * h + owner_side) * dp_count + p
                        perm.append((source, target))
            outgoing = lax.dynamic_index_in_dim(
                kept, (side_index + step) % side_count, axis=0, keepdims=False
            )
            arrived = lax.ppermute(outgoing, ALL, perm)
            grad_w_out = arrived if grad_w_out is None else grad_w_out + arrived
    else:
        pieces = partial.reshape(chunk_count, chunk, width)
        holder = side_index * dp_count + dp_index
        grad_w_out = None
        for step in range(chunk_count):
            perm = []
            for g in range(side_count):
                for h in range(head_count):
                    for p in range(dp_count):
                        c = (g * dp_count + p + step) % chunk_count
                        source = (g * head_count + h) * dp_count + p
                        target = (side_count * h + c // dp_count) * dp_count + c % dp_count
                        perm.append((source, target))
            outgoing = lax.dynamic_index_in_dim(
                pieces, (holder + step) % chunk_count, axis=0, keepdims=False
            )
            arrived = lax.ppermute(outgoing, ALL, perm)
            grad_w_out = arrived if grad_w_out is None else grad_w_out + arrived
    return (projected.reshape(1, row_count, width), grad_w_out)


def solution(mesh):
    seq_count = mesh.shape["seq"]
    dp_count = mesh.shape["dp"]
    fine = Mesh(mesh.devices.reshape(seq_count // HEADS, HEADS, dp_count), ("side", "inner", "dp"))
    seq = ("side", "inner")
    placed = (
        P("dp", seq, None),
        P("dp", seq, None),
        P("dp", seq, None),
        P(ALL, None),
        P("dp", seq, None),
    )
    return jax.shard_map(
        local,
        mesh=fine,
        in_specs=placed,
        out_specs=(P("dp", seq, None), P(ALL, None)),
        check_vma=False,
    )
```

profile of v0, /device:TPU:1, one launch (start us, length us, event | category | flops | bytes accessed | tf_op | source)
XLA Modules:
  0.0 170.2 jit_solution(15018882049853274398)
XLA Ops:
  7.9 1.7 %reshape_squeeze.9 = bf16[192,8,192]{2,1,0:T(8,128)(2,1)S(1)} reshape(bf16[1,192,1536]{2,1,0:T(8,128)(2,1)} %param.8) | data formatting | bytes 1179648 | tf_op jit(solution)/shard_map/reshape;squeeze | solution.py:55
  11.5 2.0 %pad_maximum_fusion = bf16[192,8,576]{2,0,1:T(8,128)(2,1)} fusion(bf16[192,8,192]{2,0,1:T(8,128)(2,1)S(1)} %copy.13, bf16[192,8,192]{2,0,1:T(8,128)(2,1)S(1)} %copy.12, bf16[192,8,192]{2,0,1:T(8,128)(2,1)S(1)} %copy.14), kind=kLoop, calls=%fused_computation.20 | loop fusion | flops 5308416 | bytes 3538944 | tf_op jit(solution)/shard_map/concatenate | solution.py:74
  13.5 5.3 %all-to-all-start = ((bf16[192,8,576]{2,0,1:T(8,128)(2,1)}), bf16[192,8,576]{2,0,1:T(8,128)(2,1)S(1)}, u32[]{:S(2)}, u32[]{:S(2)}) async-start(bf16[192,8,576]{2,0,1:T(8,128)(2,1)} %pad_maximum_fusion), calls=%async_computation | async-start | bytes 3932160 | tf_op jit(solution)/shard_map/all_to_all | solution.py:75
  18.8 0.7 all-gather.4.cloned.1.call-update
  19.7 1.2 fusion.41
  20.9 2.3 %collective-permute-start = (bf16[192,384]{1,0:T(8,128)(2,1)}, bf16[192,384]{1,0:T(8,128)(2,1)}, u32[]{:S(2)}, u32[]{:S(2)}) collective-permute-start(bf16[192,384]{1,0:T(8,128)(2,1)} %get-tuple-element.63), channel_id=1, source_target_pairs={{0,16},{2,18},{4,20},{6,22},{8,24},{10,26},{12,28},{14,30},{16,0},... | collective-permute-start | bytes 442376 | tf_op jit(solution)/shard_map/ppermute | solution.py:73
  23.2 1.7 collective-permute-start.1
  24.9 2.3 %collective-permute-start.2 = (bf16[192,384]{1,0:T(8,128)(2,1)}, bf16[192,384]{1,0:T(8,128)(2,1)}, u32[]{:S(2)}, u32[]{:S(2)}) collective-permute-start(bf16[192,384]{1,0:T(8,128)(2,1)} %get-tuple-element.65), channel_id=1, source_target_pairs={{0,20},{2,22},{4,24},{6,26},{8,28},{10,30},{12,16},{14,18},{16,4},... | collective-permute-start | bytes 442376 | tf_op jit(solution)/shard_map/ppermute | solution.py:73
  27.2 1.2 collective-permute-start.3
  28.4 2.1 %collective-permute-start.4 = (bf16[192,384]{1,0:T(8,128)(2,1)}, bf16[192,384]{1,0:T(8,128)(2,1)}, u32[]{:S(2)}, u32[]{:S(2)}) collective-permute-start(bf16[192,384]{1,0:T(8,128)(2,1)} %get-tuple-element.67), channel_id=1, source_target_pairs={{0,24},{2,26},{4,28},{6,30},{8,16},{10,18},{12,20},{14,22},{16,8},... | collective-permute-start | bytes 442376 | tf_op jit(solution)/shard_map/ppermute | solution.py:73
  30.5 0.9 fusion.34
  31.4 30.7 %collective-permute-done = bf16[192,384]{1,0:T(8,128)(2,1)} collective-permute-done((bf16[192,384]{1,0:T(8,128)(2,1)}, bf16[192,384]{1,0:T(8,128)(2,1)}, u32[]{:S(2)}, u32[]{:S(2)}) %collective-permute-start) | collective-permute-done | bytes 147488 | tf_op jit(solution)/shard_map/ppermute | solution.py:73
  62.1 4.1 %collective-permute-start.7 = (bf16[192,384]{1,0:T(8,128)(2,1)}, bf16[192,384]{1,0:T(8,128)(2,1)S(1)}, u32[]{:S(2)}, u32[]{:S(2)}) collective-permute-start(bf16[192,384]{1,0:T(8,128)(2,1)} %get-tuple-element.62), channel_id=1, source_target_pairs={{0,30},{2,16},{4,18},{6,20},{8,22},{10,24},{12,26},{14,28},{16,14}... | collective-permute-start | bytes 442376 | tf_op jit(solution)/shard_map/ppermute | solution.py:73
  66.2 4.9 %collective-permute-start.5 = (bf16[192,384]{1,0:T(8,128)(2,1)}, bf16[192,384]{1,0:T(8,128)(2,1)S(1)}, u32[]{:S(2)}, u32[]{:S(2)}) collective-permute-start(bf16[192,384]{1,0:T(8,128)(2,1)} %get-tuple-element.69), channel_id=1, source_target_pairs={{0,26},{2,28},{4,30},{6,16},{8,18},{10,20},{12,22},{14,24},{16,10}... | collective-permute-start | bytes 442376 | tf_op jit(solution)/shard_map/ppermute | solution.py:73
  71.1 2.7 %collective-permute-done.2 = bf16[192,384]{1,0:T(8,128)(2,1)} collective-permute-done((bf16[192,384]{1,0:T(8,128)(2,1)}, bf16[192,384]{1,0:T(8,128)(2,1)}, u32[]{:S(2)}, u32[]{:S(2)}) %collective-permute-start.2) | collective-permute-done | bytes 147488 | tf_op jit(solution)/shard_map/ppermute | solution.py:73
  73.7 3.9 %collective-permute-done.3 = bf16[192,384]{1,0:T(8,128)(2,1)} collective-permute-done((bf16[192,384]{1,0:T(8,128)(2,1)}, bf16[192,384]{1,0:T(8,128)(2,1)}, u32[]{:S(2)}, u32[]{:S(2)}) %collective-permute-start.3) | collective-permute-done | bytes 147488 | tf_op jit(solution)/shard_map/ppermute | solution.py:73
  77.6 1.6 collective-permute-done.4
  79.2 13.2 %collective-permute-done.7 = bf16[192,384]{1,0:T(8,128)(2,1)S(1)} collective-permute-done((bf16[192,384]{1,0:T(8,128)(2,1)}, bf16[192,384]{1,0:T(8,128)(2,1)S(1)}, u32[]{:S(2)}, u32[]{:S(2)}) %collective-permute-start.7) | collective-permute-done | bytes 147488 | tf_op jit(solution)/shard_map/ppermute | solution.py:73
  92.4 7.3 %collective-permute-done.6 = bf16[192,384]{1,0:T(8,128)(2,1)S(1)} collective-permute-done((bf16[192,384]{1,0:T(8,128)(2,1)}, bf16[192,384]{1,0:T(8,128)(2,1)S(1)}, u32[]{:S(2)}, u32[]{:S(2)}) %collective-permute-start.6) | collective-permute-done | bytes 147488 | tf_op jit(solution)/shard_map/ppermute | solution.py:73
  100.9 0.9 constant_dynamic-update-slice_fusion.7
  101.8 0.9 constant_dynamic-update-slice_fusion.6
  102.7 0.9 constant_dynamic-update-slice_fusion.5
  103.7 0.9 constant_dynamic-update-slice_fusion.4
  104.6 0.9 constant_dynamic-update-slice_fusion.3
  105.7 1.9 %fusion.42 = (bf16[3072,192]{1,0:T(8,128)(2,1)}, bf16[3072,192]{1,0:T(8,128)(2,1)S(1)}) fusion(bf16[3072,384]{1,0:T(8,128)(2,1)S(1)} %constant_dynamic-update-slice_fusion), kind=kLoop, calls=%fused_computation.66 | loop fusion | bytes 4718592 | tf_op jit(solution)/shard_map/slice | solution.py:84
  107.6 12.0 %while.10 = (s32[]{:T(128)}, bf16[3,512,192]{1,2,0:T(8,128)(2,1)S(1)}, bf16[3,512,192]{2,1,0:T(8,128)(2,1)S(1)}, bf16[3072,192]{1,0:T(8,128)(2,1)S(1)}, bf16[3072,192]{1,0:T(8,128)(2,1)}, /*index=5*/s32[]{:T(128)}) while((s32[]{:T(128)}, bf16[3,512,192]{1,2,0:T(8,128)(2,1)S(1)}, bf16[3,512,192]{2,1,0:T(8,128)(2,1)S(1)}, ...), condition=%wide.region_3.4_spmd, body=%wide.region_0.3_spmd.sunk | while | flops 1220738048 | bytes 27207784 | solution.py:26
  107.6 1.1 multiply_reduce_fusion.2
  108.7 1.2 fusion.56
  110.1 1.5 fusion.57
  111.6 1.1 multiply_reduce_fusion.2
  112.7 1.2 fusion.56
  114.1 1.5 fusion.57
  115.6 1.1 multiply_reduce_fusion.2
  116.7 1.2 fusion.56
  118.1 1.5 fusion.57
  119.6 1.2 copy.17
  120.8 5.1 %all-to-all-start.1 = ((bf16[8,192,192]{2,1,0:T(8,128)(2,1)}), bf16[8,192,192]{2,1,0:T(8,128)(2,1)S(1)}, u32[]{:S(2)}, u32[]{:S(2)}) async-start(bf16[8,192,192]{2,1,0:T(8,128)(2,1)} %bitcast.14), calls=%async_computation.1 | async-start | bytes 1572864 | tf_op jit(solution)/shard_map/all_to_all | solution.py:47
  126.0 3.4 %fusion.23 = f32[2,2,48,1536]{3,2,1,0:T(8,128)S(1)} fusion(bf16[2,2,48,1536]{3,2,1,0:T(8,128)(2,1)S(1)} %bitcast.73, bf16[1,1536,1536]{2,1,0:T(8,128)(2,1)} %all-gather.6.cloned.1.call-done), kind=kOutput, calls=%fused_computation.16 | convolution fusion | flops 905969664 | bytes 6488064 | tf_op jit(solution)/shard_map/dot_general | solution.py:86
  129.4 1.3 collective-permute-start.8
  130.7 9.3 %all-to-all-done.1 = bf16[8,192,192]{2,1,0:T(8,128)(2,1)S(1)} async-done(((bf16[8,192,192]{2,1,0:T(8,128)(2,1)}), bf16[8,192,192]{2,1,0:T(8,128)(2,1)S(1)}, u32[]{:S(2)}, u32[]{:S(2)}) %all-to-all-start.1) | async-done | bytes 589856 | tf_op jit(solution)/shard_map/all_to_all | solution.py:47
  140.5 1.5 reshape.26
  142.0 2.5 %collective-permute-done.8 = f32[2,48,1536]{2,1,0:T(8,128)} collective-permute-done((f32[2,48,1536]{2,1,0:T(8,128)S(1)}, f32[2,48,1536]{2,1,0:T(8,128)}, u32[]{:S(2)}, u32[]{:S(2)}) %collective-permute-start.8) | collective-permute-done | bytes 589856 | tf_op jit(solution)/shard_map/ppermute | solution.py:99
  144.5 1.1 bitcast_add_fusion
  145.7 1.1 collective-permute-start.10
  146.8 3.4 %collective-permute-start.9 = (f32[48,1536]{1,0:T(8,128)S(1)}, f32[48,1536]{1,0:T(8,128)S(1)}, u32[]{:S(2)}, u32[]{:S(2)}) collective-permute-start(f32[48,1536]{1,0:T(8,128)S(1)} %get-tuple-element.71), channel_id=1, source_target_pairs={{0,0},{1,1},{2,4},{3,5},{4,8},{5,9},{6,12},{7,13},{8,16},{9,17},{1... | collective-permute-start | bytes 884744 | tf_op jit(solution)/shard_map/ppermute | solution.py:113
  150.2 4.2 %fusion.25 = bf16[1,192,1536]{2,1,0:T(8,128)(2,1)} fusion(bf16[192,1536]{1,0:T(8,128)(2,1)S(1)} %copy-done.3, bf16[1536,1536]{1,0:T(8,128)(2,1)} %all-gather.4.cloned.1.call-done), kind=kOutput, calls=%fused_computation.19 | convolution fusion | flops 906264576 | bytes 5898240 | tf_op jit(solution)/shard_map/dot_general | solution.py:91
  154.4 8.2 %collective-permute-done.9 = f32[48,1536]{1,0:T(8,128)S(1)} collective-permute-done((f32[48,1536]{1,0:T(8,128)S(1)}, f32[48,1536]{1,0:T(8,128)S(1)}, u32[]{:S(2)}, u32[]{:S(2)}) %collective-permute-start.9) | collective-permute-done | bytes 294944 | tf_op jit(solution)/shard_map/ppermute | solution.py:113
  162.6 0.7 add.135
  (45 shorter events, 5.1 us)
Async XLA Ops:
  7.2 2.7 %copy-start.1 = (bf16[1,192,1536]{2,1,0:T(8,128)(2,1)S(1)}, bf16[1,192,1536]{2,1,0:T(8,128)(2,1)}, u32[]{:S(2)}) copy-start(bf16[1,192,1536]{2,1,0:T(8,128)(2,1)} %param.9) | copy-start | bytes 1769476
  7.2 118.8 %all-gather.6.cloned.1.call-start = ((), (), s32[]{:S(2)}) async-start(), calls=%async_computation.3 | async-start | bytes 5308416 | tf_op jit(solution)/shard_map/all_gather | solution.py:44
  9.6 1.1 copy-start.2
  13.5 86.1 %all-to-all-start = ((bf16[192,8,576]{2,0,1:T(8,128)(2,1)}), bf16[192,8,576]{2,0,1:T(8,128)(2,1)S(1)}, u32[]{:S(2)}, u32[]{:S(2)}) async-start(bf16[192,8,576]{2,0,1:T(8,128)(2,1)} %pad_maximum_fusion), calls=%async_computation | async-start | bytes 3932160 | tf_op jit(solution)/shard_map/all_to_all | solution.py:75
  18.8 131.3 %all-gather.4.cloned.1.call-start = ((), (), s32[]{:S(2)}) async-start(), calls=%async_computation.2 | async-start | bytes 4866048 | tf_op jit(solution)/shard_map/all_gather | solution.py:43
  20.9 41.2 %collective-permute-start = (bf16[192,384]{1,0:T(8,128)(2,1)}, bf16[192,384]{1,0:T(8,128)(2,1)}, u32[]{:S(2)}, u32[]{:S(2)}) collective-permute-start(bf16[192,384]{1,0:T(8,128)(2,1)} %get-tuple-element.63), channel_id=1, source_target_pairs={{0,16},{2,18},{4,20},{6,22},{8,24},{10,26},{12,28},{14,30},{16,0},... | collective-permute-start | bytes 442376 | tf_op jit(solution)/shard_map/ppermute | solution.py:73
  23.2 43.0 %collective-permute-start.1 = (bf16[192,384]{1,0:T(8,128)(2,1)}, bf16[192,384]{1,0:T(8,128)(2,1)}, u32[]{:S(2)}, u32[]{:S(2)}) collective-permute-start(bf16[192,384]{1,0:T(8,128)(2,1)} %get-tuple-element.64), channel_id=1, source_target_pairs={{0,18},{2,20},{4,22},{6,24},{8,26},{10,28},{12,30},{14,16},{16,2},... | collective-permute-start | bytes 442376 | tf_op jit(solution)/shard_map/ppermute | solution.py:73
  24.9 48.8 %collective-permute-start.2 = (bf16[192,384]{1,0:T(8,128)(2,1)}, bf16[192,384]{1,0:T(8,128)(2,1)}, u32[]{:S(2)}, u32[]{:S(2)}) collective-permute-start(bf16[192,384]{1,0:T(8,128)(2,1)} %get-tuple-element.65), channel_id=1, source_target_pairs={{0,20},{2,22},{4,24},{6,26},{8,28},{10,30},{12,16},{14,18},{16,4},... | collective-permute-start | bytes 442376 | tf_op jit(solution)/shard_map/ppermute | solution.py:73
  27.2 50.4 %collective-permute-start.3 = (bf16[192,384]{1,0:T(8,128)(2,1)}, bf16[192,384]{1,0:T(8,128)(2,1)}, u32[]{:S(2)}, u32[]{:S(2)}) collective-permute-start(bf16[192,384]{1,0:T(8,128)(2,1)} %get-tuple-element.66), channel_id=1, source_target_pairs={{0,22},{2,24},{4,26},{6,28},{8,30},{10,16},{12,18},{14,20},{16,6},... | collective-permute-start | bytes 442376 | tf_op jit(solution)/shard_map/ppermute | solution.py:73
  28.4 50.8 %collective-permute-start.4 = (bf16[192,384]{1,0:T(8,128)(2,1)}, bf16[192,384]{1,0:T(8,128)(2,1)}, u32[]{:S(2)}, u32[]{:S(2)}) collective-permute-start(bf16[192,384]{1,0:T(8,128)(2,1)} %get-tuple-element.67), channel_id=1, source_target_pairs={{0,24},{2,26},{4,28},{6,30},{8,16},{10,18},{12,20},{14,22},{16,8},... | collective-permute-start | bytes 442376 | tf_op jit(solution)/shard_map/ppermute | solution.py:73
  62.1 30.3 %collective-permute-start.7 = (bf16[192,384]{1,0:T(8,128)(2,1)}, bf16[192,384]{1,0:T(8,128)(2,1)S(1)}, u32[]{:S(2)}, u32[]{:S(2)}) collective-permute-start(bf16[192,384]{1,0:T(8,128)(2,1)} %get-tuple-element.62), channel_id=1, source_target_pairs={{0,30},{2,16},{4,18},{6,20},{8,22},{10,24},{12,26},{14,28},{16,14}... | collective-permute-start | bytes 442376 | tf_op jit(solution)/shard_map/ppermute | solution.py:73
  66.2 26.2 %collective-permute-start.5 = (bf16[192,384]{1,0:T(8,128)(2,1)}, bf16[192,384]{1,0:T(8,128)(2,1)S(1)}, u32[]{:S(2)}, u32[]{:S(2)}) collective-permute-start(bf16[192,384]{1,0:T(8,128)(2,1)} %get-tuple-element.69), channel_id=1, source_target_pairs={{0,26},{2,28},{4,30},{6,16},{8,18},{10,20},{12,22},{14,24},{16,10}... | collective-permute-start | bytes 442376 | tf_op jit(solution)/shard_map/ppermute | solution.py:73
  73.7 25.9 %collective-permute-start.6 = (bf16[192,384]{1,0:T(8,128)(2,1)}, bf16[192,384]{1,0:T(8,128)(2,1)S(1)}, u32[]{:S(2)}, u32[]{:S(2)}) collective-permute-start(bf16[192,384]{1,0:T(8,128)(2,1)} %get-tuple-element.68), channel_id=1, source_target_pairs={{0,28},{2,30},{4,16},{6,18},{8,20},{10,22},{12,24},{14,26},{16,12}... | collective-permute-start | bytes 442376 | tf_op jit(solution)/shard_map/ppermute | solution.py:73
  92.4 7.3 %copy-start.4 = (bf16[192,384]{1,0:T(8,128)(2,1)}, bf16[192,384]{1,0:T(8,128)(2,1)S(1)}, u32[]{:S(2)}) copy-start(bf16[192,384]{1,0:T(8,128)(2,1)S(1)} %collective-permute-done.5) | copy-start | bytes 442372
  99.6 0.7 copy-start.6
  100.3 5.2 %copy-start.5 = (bf16[192,384]{1,0:T(8,128)(2,1)S(1)}, bf16[192,384]{1,0:T(8,128)(2,1)}, u32[]{:S(2)}) copy-start(bf16[192,384]{1,0:T(8,128)(2,1)} %copy-done.4) | copy-start | bytes 442372
  100.4 5.2 %copy-start.7 = (bf16[192,384]{1,0:T(8,128)(2,1)S(1)}, bf16[192,384]{1,0:T(8,128)(2,1)}, u32[]{:S(2)}) copy-start(bf16[192,384]{1,0:T(8,128)(2,1)} %copy-done.6) | copy-start | bytes 442372
  108.7 1.4 copy-start
  112.7 1.4 copy-start
  116.7 1.4 copy-start
  120.8 19.2 %all-to-all-start.1 = ((bf16[8,192,192]{2,1,0:T(8,128)(2,1)}), bf16[8,192,192]{2,1,0:T(8,128)(2,1)S(1)}, u32[]{:S(2)}, u32[]{:S(2)}) async-start(bf16[8,192,192]{2,1,0:T(8,128)(2,1)} %bitcast.14), calls=%async_computation.1 | async-start | bytes 1572864 | tf_op jit(solution)/shard_map/all_to_all | solution.py:47
  129.4 15.1 %collective-permute-start.8 = (f32[2,48,1536]{2,1,0:T(8,128)S(1)}, f32[2,48,1536]{2,1,0:T(8,128)}, u32[]{:S(2)}, u32[]{:S(2)}) collective-permute-start(f32[2,48,1536]{2,1,0:T(8,128)S(1)} %dynamic-slice_bitcast_fusion), channel_id=1, source_target_pairs={{0,1},{1,0},{2,3},{3,2},{4,5},{5,4},{6,7},{7,6},{8,9},{9,8},{10,11... | collective-permute-start | bytes 1769480 | tf_op jit(solution)/shard_map/ppermute | solution.py:99
  142.0 8.2 %copy-start.3 = (bf16[192,1536]{1,0:T(8,128)(2,1)S(1)}, bf16[192,1536]{1,0:T(8,128)(2,1)}, u32[]{:S(2)}) copy-start(bf16[192,1536]{1,0:T(8,128)(2,1)} %reshape.26) | copy-start | bytes 1769476
  145.7 8.7 %collective-permute-start.10 = (f32[48,1536]{1,0:T(8,128)S(1)}, f32[48,1536]{1,0:T(8,128)S(1)}, u32[]{:S(2)}, u32[]{:S(2)}) collective-permute-start(f32[48,1536]{1,0:T(8,128)S(1)} %get-tuple-element.70), channel_id=1, source_target_pairs={{0,2},{1,3},{2,6},{3,7},{4,10},{5,11},{6,14},{7,15},{8,18},{9,19},... | collective-permute-start | bytes 884744 | tf_op jit(solution)/shard_map/ppermute | solution.py:113
  146.8 15.8 %collective-permute-start.9 = (f32[48,1536]{1,0:T(8,128)S(1)}, f32[48,1536]{1,0:T(8,128)S(1)}, u32[]{:S(2)}, u32[]{:S(2)}) collective-permute-start(f32[48,1536]{1,0:T(8,128)S(1)} %get-tuple-element.71), channel_id=1, source_target_pairs={{0,0},{1,1},{2,4},{3,5},{4,8},{5,9},{6,12},{7,13},{8,16},{9,17},{1... | collective-permute-start | bytes 884744 | tf_op jit(solution)/shard_map/ppermute | solution.py:113
Sparse Core Ops, SparseCore 0:
  9.6 63.7 all-gather.5
  76.3 72.7 all-gather.3
where the time goes:
time: 171 us; the launch traced here: 170 us
  waiting for transfers between devices  80.7 us (47%)
  starting transfers between devices  34.8 us (20%)
  local copies, waits for them, and re-layouts  15.4 us (9%)
  matrix products  15.4 us (9%)
  between operations  14.3 us (8%)
  other arithmetic  9.51 us (6%)
    ppermute x8, waiting for transfers between devices, local(): kv_crossed.append(lax.ppermute(outgoing, ('side', 'inner'), perm))  59.3 us
    ppermute x8, starting transfers between devices, local(): kv_crossed.append(lax.ppermute(outgoing, ('side', 'inner'), perm))  18.6 us
    all_to_all x1, waiting for transfers between devices, a2a(): lax.all_to_all(tensor, 'inner', split_axis=0, concat_axis=0, tiled=True)  9.3 us
    ppermute x2, waiting for transfers between devices, local(): arrived = lax.ppermute(outgoing, ALL, perm)  8.16 us
    unnamed x22, local copies, waits for them, and re-layouts  6 us
    all_to_all x1, starting transfers between devices, local(): lax.all_to_all(stacked, 'inner', split_axis=1, concat_axis=0, tiled=True)  5.31 us
    all_to_all x1, starting transfers between devices, a2a(): lax.all_to_all(tensor, 'inner', split_axis=0, concat_axis=0, tiled=True)  5.14 us
    dot_general x3, matrix products, one_block(): mixed = jnp.dot(weights, value_all, preferred_element_type=jnp.float32)  4.42 us
  transfers between devices with their start and end apart: 15, of which 9 were waited for; matrix products, arithmetic and copies ran while one was open for 22% of the time, Pallas kernels for 0%

commit v1 on v0

--- a/solution.py
+++ b/solution.py
@@ -72,9 +72,12 @@
             )
             kv_crossed.append(lax.ppermute(outgoing, ("side", "inner"), perm))
     stacked = jnp.concatenate([by_lane(queries), kv_raw], axis=2)
-    got = lax.all_to_all(stacked, "inner", split_axis=1, concat_axis=0, tiled=True).reshape(
-        head_count * row_count, 3 * head_width
-    )
+    got = jnp.concatenate(
+        lax.all_to_all(
+            jnp.stack(jnp.split(stacked, lax.axis_size("inner"), axis=1)), "inner", 0, 0
+        ),
+        axis=0,
+    ).reshape(head_count * row_count, 3 * head_width)
     early = len(kv_crossed)
     kv_early, got = lax.optimization_barrier((kv_crossed[:early], got))
     kv_crossed = list(kv_early) + kv_crossed[early:]

time: 171 us -> 177 us (1.035)
  local copies, waits for them, and re-layouts: 15.4 us -> 30.1 us
  waiting for transfers between devices: 80.7 us -> 67.4 us
  other arithmetic: 9.51 us -> 13.1 us
  matrix products: 15.4 us -> 18.2 us
  starting transfers between devices: 34.8 us -> 32.7 us
    ppermute x8, waiting for transfers between devices: 59.3 us -> 46.1 us  [local(): kv_crossed.append(lax.ppermute(outgoing, ('side', 'inner'), perm))]
    unnamed x22 -> x29, local copies, waits for them, and re-layouts: 6 us -> 15.4 us
    concatenate x0 -> x2, other arithmetic: none -> 5.86 us  [local(): jnp.concatenate([by_lane(key_vectors), by_lane(value_vectors)], axis=2)]
    split x0 -> x1, local copies, waits for them, and re-layouts: none -> 3.29 us  [local(): jnp.split(stacked, lax.axis_size('inner'), axis=1)]
    dot_general x3, matrix products: 3.32 us -> 6.15 us  [one_block(): jnp.dot(query_block, key_all.T, preferred_element_type=jnp.float32)]
    squeeze x2 -> x0, other arithmetic: 2.11 us -> none  [local(): lax.dynamic_index_in_dim(kv_raw, (inner_index + shift) % head_count, axis...]
    another operation x6 -> x3, local copies, waits for them, and re-layouts: 3.39 us -> 3.85 us  [by_lane(): return tensor[0].reshape(row_count, head_count, head_width)]
  transfers between devices with their start and end apart: 15 -> 15, of which waited for: 9 -> 9; matrix products, arithmetic and copies ran while one was open for 22% -> 34% of each run, Pallas kernels for 0% -> 0%
where the time goes in v1:
time: 177 us; the launch traced here: 176 us
  waiting for transfers between devices  67.4 us (38%)
  starting transfers between devices  32.7 us (18%)
  local copies, waits for them, and re-layouts  30.1 us (17%)
  matrix products  18.2 us (10%)
  between operations  14.3 us (8%)
  other arithmetic  13.1 us (7%)
    ppermute x8, waiting for transfers between devices, local(): kv_crossed.append(lax.ppermute(outgoing, ('side', 'inner'), perm))  46.1 us
    ppermute x8, starting transfers between devices, local(): kv_crossed.append(lax.ppermute(outgoing, ('side', 'inner'), perm))  17.5 us
    unnamed x29, local copies, waits for them, and re-layouts  15.4 us
    all_to_all x1, waiting for transfers between devices, a2a(): lax.all_to_all(tensor, 'inner', split_axis=0, concat_axis=0, tiled=True)  10.7 us
    ppermute x2, waiting for transfers between devices, local(): arrived = lax.ppermute(outgoing, ALL, perm)  8.09 us
    dot_general x3, matrix products, one_block(): jnp.dot(query_block, key_all.T, preferred_element_type=jnp.float32)  6.15 us
    concatenate x2, other arithmetic, local(): jnp.concatenate([by_lane(key_vectors), by_lane(value_vectors)], axis=2)  5.86 us
    all_to_all x1, starting transfers between devices, local(): lax.all_to_all(jnp.stack(jnp.split(stacked, lax.axis_size('inner'), axis=...  5.31 us
  transfers between devices with their start and end apart: 15, of which 9 were waited for; matrix products, arithmetic and copies ran while one was open for 34% of the time, Pallas kernels for 0%

profile of v1, /device:TPU:1, one launch (start us, length us, event | category | flops | bytes accessed | tf_op | source)
XLA Modules:
  0.0 176.0 jit_solution(14845971022519815148)
XLA Ops:
  7.9 1.7 reshape_squeeze.10
  10.3 1.5 reshape_squeeze.11
  11.8 1.9 %pad_maximum_fusion = bf16[192,8,576]{2,1,0:T(8,128)(2,1)S(1)} fusion(bf16[192,8,192]{2,1,0:T(8,128)(2,1)S(1)} %reshape_squeeze.10, bf16[192,8,192]{2,1,0:T(8,128)(2,1)S(1)} %reshape_squeeze.9, bf16[192,8,192]{2,1,0:T(8,128)(2,1)} %reshape_squeeze.11), kind=kLoop, calls=%fused_computation.20 | loop fusion | flops 5308416 | bytes 3538944 | tf_op jit(solution)/shard_map/concatenate | solution.py:74
  13.7 3.3 %fusion.35 = (bf16[192,1,576]{2,1,0:T(2,128)(2,1)S(1)}, bf16[192,1,576]{2,1,0:T(2,128)(2,1)S(1)}, bf16[192,1,576]{2,1,0:T(2,128)(2,1)S(1)}, bf16[192,1,576]{2,1,...) fusion(bf16[192,8,576]{2,1,0:T(8,128)(2,1)S(1)} %pad_maximum_fusion), kind=kLoop, calls=%fused_computation.75 | loop fusion | bytes 3538944 | tf_op jit(solution)/shard_map/split | solution.py:77
  22.8 5.3 %all-to-all-start = ((bf16[8,192,1,576]{3,1,2,0:T(8,128)(2,1)}), bf16[8,192,1,576]{3,1,2,0:T(8,128)(2,1)S(1)}, u32[]{:S(2)}, u32[]{:S(2)}) async-start(bf16[8,192,1,576]{3,1,2,0:T(8,128)(2,1)} %bitcast_dynamic-update-slice_fusion), calls=%async_computation | async-start | bytes 3932160 | tf_op jit(solution)/shard_map/all_to_all | solution.py:76
  28.9 4.7 %fusion.26 = (bf16[192,1,384]{2,1,0:T(2,128)(2,1)}, bf16[192,1,384]{2,1,0:T(2,128)(2,1)S(1)}, bf16[192,1,384]{2,1,0:T(2,128)(2,1)S(1)}, bf16[192,1,384]{2,1,0:T(...) fusion(s32[]{:T(128)S(6)} %select_n.97, bf16[192,8,192]{2,1,0:T(8,128)(2,1)S(1)} %reshape_squeeze.9, ...), kind=kLoop, calls=%fused_computation.40 | loop fusion | flops 1769472 | bytes 2064408 | tf_op jit(solution)/shard_map/concatenate | solution.py:57
  34.3 2.3 %collective-permute-start = (bf16[192,384]{1,0:T(8,128)(2,1)}, bf16[192,384]{1,0:T(8,128)(2,1)}, u32[]{:S(2)}, u32[]{:S(2)}) collective-permute-start(bf16[192,384]{1,0:T(8,128)(2,1)} %bitcast.80), channel_id=1, source_target_pairs={{0,16},{2,18},{4,20},{6,22},{8,24},{10,26},{12,28},{14,30},{16,0},... | collective-permute-start | bytes 442376 | tf_op jit(solution)/shard_map/ppermute | solution.py:73
  37.3 1.7 collective-permute-start.1
  39.7 2.3 %collective-permute-start.2 = (bf16[192,384]{1,0:T(8,128)(2,1)}, bf16[192,384]{1,0:T(8,128)(2,1)}, u32[]{:S(2)}, u32[]{:S(2)}) collective-permute-start(bf16[192,384]{1,0:T(8,128)(2,1)} %bitcast.78), channel_id=1, source_target_pairs={{0,20},{2,22},{4,24},{6,26},{8,28},{10,30},{12,16},{14,18},{16,4},... | collective-permute-start | bytes 442376 | tf_op jit(solution)/shard_map/ppermute | solution.py:73
  42.7 1.2 collective-permute-start.3
  44.6 2.1 %collective-permute-start.4 = (bf16[192,384]{1,0:T(8,128)(2,1)}, bf16[192,384]{1,0:T(8,128)(2,1)}, u32[]{:S(2)}, u32[]{:S(2)}) collective-permute-start(bf16[192,384]{1,0:T(8,128)(2,1)} %bitcast.76), channel_id=1, source_target_pairs={{0,24},{2,26},{4,28},{6,30},{8,16},{10,18},{12,20},{14,22},{16,8},... | collective-permute-start | bytes 442376 | tf_op jit(solution)/shard_map/ppermute | solution.py:73
  46.7 1.6 copy.126
  48.3 1.2 fusion.33
  49.5 14.4 %collective-permute-done = bf16[192,384]{1,0:T(8,128)(2,1)} collective-permute-done((bf16[192,384]{1,0:T(8,128)(2,1)}, bf16[192,384]{1,0:T(8,128)(2,1)}, u32[]{:S(2)}, u32[]{:S(2)}) %collective-permute-start) | collective-permute-done | bytes 147488 | tf_op jit(solution)/shard_map/ppermute | solution.py:73
  63.9 3.5 %collective-permute-start.7 = (bf16[192,384]{1,0:T(8,128)(2,1)}, bf16[192,384]{1,0:T(8,128)(2,1)S(1)}, u32[]{:S(2)}, u32[]{:S(2)}) collective-permute-start(bf16[192,384]{1,0:T(8,128)(2,1)} %bitcast.73), channel_id=1, source_target_pairs={{0,30},{2,16},{4,18},{6,20},{8,22},{10,24},{12,26},{14,28},{16,14}... | collective-permute-start | bytes 442376 | tf_op jit(solution)/shard_map/ppermute | solution.py:73
  67.4 4.4 %collective-permute-start.5 = (bf16[192,384]{1,0:T(8,128)(2,1)S(1)}, bf16[192,384]{1,0:T(8,128)(2,1)S(1)}, u32[]{:S(2)}, u32[]{:S(2)}) collective-permute-start(bf16[192,384]{1,0:T(8,128)(2,1)S(1)} %bitcast.96), channel_id=1, source_target_pairs={{0,26},{2,28},{4,30},{6,16},{8,18},{10,20},{12,22},{14,24},{16,10}... | collective-permute-start | bytes 442376 | tf_op jit(solution)/shard_map/ppermute | solution.py:73
  71.9 3.3 %collective-permute-done.2 = bf16[192,384]{1,0:T(8,128)(2,1)} collective-permute-done((bf16[192,384]{1,0:T(8,128)(2,1)}, bf16[192,384]{1,0:T(8,128)(2,1)}, u32[]{:S(2)}, u32[]{:S(2)}) %collective-permute-start.2) | collective-permute-done | bytes 147488 | tf_op jit(solution)/shard_map/ppermute | solution.py:73
  75.1 3.3 %collective-permute-done.3 = bf16[192,384]{1,0:T(8,128)(2,1)} collective-permute-done((bf16[192,384]{1,0:T(8,128)(2,1)}, bf16[192,384]{1,0:T(8,128)(2,1)}, u32[]{:S(2)}, u32[]{:S(2)}) %collective-permute-start.3) | collective-permute-done | bytes 147488 | tf_op jit(solution)/shard_map/ppermute | solution.py:73
  78.4 1.8 %collective-permute-done.4 = bf16[192,384]{1,0:T(8,128)(2,1)} collective-permute-done((bf16[192,384]{1,0:T(8,128)(2,1)}, bf16[192,384]{1,0:T(8,128)(2,1)}, u32[]{:S(2)}, u32[]{:S(2)}) %collective-permute-start.4) | collective-permute-done | bytes 147488 | tf_op jit(solution)/shard_map/ppermute | solution.py:73
  80.2 16.7 %collective-permute-done.7 = bf16[192,384]{1,0:T(8,128)(2,1)S(1)} collective-permute-done((bf16[192,384]{1,0:T(8,128)(2,1)}, bf16[192,384]{1,0:T(8,128)(2,1)S(1)}, u32[]{:S(2)}, u32[]{:S(2)}) %collective-permute-start.7) | collective-permute-done | bytes 147488 | tf_op jit(solution)/shard_map/ppermute | solution.py:73
  96.9 6.7 %collective-permute-done.6 = bf16[192,384]{1,0:T(8,128)(2,1)S(1)} collective-permute-done((bf16[192,384]{1,0:T(8,128)(2,1)S(1)}, bf16[192,384]{1,0:T(8,128)(2,1)S(1)}, u32[]{:S(2)}, u32[]{:S(2)}) %collective-permute-start.6) | collective-permute-done | bytes 147488 | tf_op jit(solution)/shard_map/ppermute | solution.py:73
  104.9 0.9 constant_dynamic-update-slice_fusion.7
  105.9 0.9 constant_dynamic-update-slice_fusion.6
  106.8 0.9 constant_dynamic-update-slice_fusion.5
  107.7 0.9 constant_dynamic-update-slice_fusion.4
  109.7 1.9 %fusion.34 = (bf16[3072,192]{1,0:T(8,128)(2,1)}, bf16[3072,192]{1,0:T(8,128)(2,1)S(1)}) fusion(bf16[3072,384]{1,0:T(8,128)(2,1)S(1)} %constant_dynamic-update-slice_fusion), kind=kLoop, calls=%fused_computation.74 | loop fusion | bytes 4718592 | tf_op jit(solution)/shard_map/slice | solution.py:87
  111.6 14.9 %while.10 = (s32[]{:T(128)}, bf16[3,512,192]{1,2,0:T(8,128)(2,1)S(1)}, bf16[3,512,192]{2,1,0:T(8,128)(2,1)}, bf16[3072,192]{1,0:T(8,128)(2,1)S(1)}, bf16[3072,192]{1,0:T(8,128)(2,1)}, /*index=5*/s32[]{:T(128)}) while((s32[]{:T(128)}, bf16[3,512,192]{1,2,0:T(8,128)(2,1)S(1)}, bf16[3,512,192]{2,1,0:T(8,128)(2,1)}, ...), condition=%wide.region_3.4_spmd, body=%wide.region_0.3_spmd.sunk | while | flops 1220738048 | bytes 26815076 | solution.py:26
  111.6 2.0 %multiply_reduce_fusion.2 = (f32[512]{0:T(512)S(1)}, f32[512,3072]{1,0:T(8,128)S(1)}) fusion(bf16[3072,192]{1,0:T(8,128)(2,1)S(1)} %get-tuple-element.130, bf16[3,512,192]{2,1,0:T(8,128)(2,1)} %get-tuple-element.129, s32[]{:T(128)} %get-tuple-element.121), kind=kOutput, calls=%fused_computation.1.clone.1 | convolution fusion | flops 607124992 | bytes 7735808 | tf_op jit(solution)/shard_map/while/body/eval_jaxpr/dot_general | solution.py:18
  113.7 1.2 fusion.49
  115.1 1.5 fusion.50
  116.6 2.1 %multiply_reduce_fusion.2 = (f32[512]{0:T(512)S(1)}, f32[512,3072]{1,0:T(8,128)S(1)}) fusion(bf16[3072,192]{1,0:T(8,128)(2,1)S(1)} %get-tuple-element.130, bf16[3,512,192]{2,1,0:T(8,128)(2,1)} %get-tuple-element.129, s32[]{:T(128)} %get-tuple-element.121), kind=kOutput, calls=%fused_computation.1.clone.1 | convolution fusion | flops 607124992 | bytes 7735808 | tf_op jit(solution)/shard_map/while/body/eval_jaxpr/dot_general | solution.py:18
  118.6 1.2 fusion.49
  120.1 1.5 fusion.50
  121.5 2.1 %multiply_reduce_fusion.2 = (f32[512]{0:T(512)S(1)}, f32[512,3072]{1,0:T(8,128)S(1)}) fusion(bf16[3072,192]{1,0:T(8,128)(2,1)S(1)} %get-tuple-element.130, bf16[3,512,192]{2,1,0:T(8,128)(2,1)} %get-tuple-element.129, s32[]{:T(128)} %get-tuple-element.121), kind=kOutput, calls=%fused_computation.1.clone.1 | convolution fusion | flops 607124992 | bytes 7735808 | tf_op jit(solution)/shard_map/while/body/eval_jaxpr/dot_general | solution.py:18
  123.6 1.2 fusion.49
  125.0 1.5 fusion.50
  126.5 1.2 copy.89
  127.7 4.0 %all-to-all-start.1 = ((bf16[8,192,192]{2,1,0:T(8,128)(2,1)}), bf16[8,192,192]{2,1,0:T(8,128)(2,1)S(1)}, u32[]{:S(2)}, u32[]{:S(2)}) async-start(bf16[8,192,192]{2,1,0:T(8,128)(2,1)} %bitcast.4), calls=%async_computation.1 | async-start | bytes 1572864 | tf_op jit(solution)/shard_map/all_to_all | solution.py:47
  131.7 3.4 %fusion.23 = f32[2,2,48,1536]{3,2,1,0:T(8,128)S(1)} fusion(bf16[2,2,48,1536]{3,2,1,0:T(8,128)(2,1)S(1)} %bitcast.93, bf16[1,1536,1536]{2,1,0:T(8,128)(2,1)} %all-gather.6.cloned.1.call-done), kind=kOutput, calls=%fused_computation.16 | convolution fusion | flops 905969664 | bytes 6488064 | tf_op jit(solution)/shard_map/dot_general | solution.py:89
  135.2 1.2 collective-permute-start.8
  136.4 10.7 %all-to-all-done.1 = bf16[8,192,192]{2,1,0:T(8,128)(2,1)S(1)} async-done(((bf16[8,192,192]{2,1,0:T(8,128)(2,1)}), bf16[8,192,192]{2,1,0:T(8,128)(2,1)S(1)}, u32[]{:S(2)}, u32[]{:S(2)}) %all-to-all-start.1) | async-done | bytes 589856 | tf_op jit(solution)/shard_map/all_to_all | solution.py:47
  147.6 1.5 reshape.21
  149.1 1.1 collective-permute-done.8
  150.2 1.1 bitcast_add_fusion
  151.4 1.2 collective-permute-start.10
  152.5 3.5 %collective-permute-start.9 = (f32[48,1536]{1,0:T(8,128)S(1)}, f32[48,1536]{1,0:T(8,128)S(1)}, u32[]{:S(2)}, u32[]{:S(2)}) collective-permute-start(f32[48,1536]{1,0:T(8,128)S(1)} %get-tuple-element.79), channel_id=1, source_target_pairs={{0,0},{1,1},{2,4},{3,5},{4,8},{5,9},{6,12},{7,13},{8,16},{9,17},{1... | collective-permute-start | bytes 884744 | tf_op jit(solution)/shard_map/ppermute | solution.py:116
  156.1 4.2 %fusion.25 = bf16[1,192,1536]{2,1,0:T(8,128)(2,1)} fusion(bf16[192,1536]{1,0:T(8,128)(2,1)S(1)} %copy-done.3, bf16[1536,1536]{1,0:T(8,128)(2,1)} %all-gather.4.cloned.1.call-done), kind=kOutput, calls=%fused_computation.19 | convolution fusion | flops 906264576 | bytes 5898240 | tf_op jit(solution)/shard_map/dot_general | solution.py:94
  160.3 8.1 %collective-permute-done.9 = f32[48,1536]{1,0:T(8,128)S(1)} collective-permute-done((f32[48,1536]{1,0:T(8,128)S(1)}, f32[48,1536]{1,0:T(8,128)S(1)}, u32[]{:S(2)}, u32[]{:S(2)}) %collective-permute-start.9) | collective-permute-done | bytes 294944 | tf_op jit(solution)/shard_map/ppermute | solution.py:116
  (51 shorter events, 15.8 us)
Async XLA Ops:
  7.2 2.5 %copy-start.1 = (bf16[1,192,1536]{2,1,0:T(8,128)(2,1)S(1)}, bf16[1,192,1536]{2,1,0:T(8,128)(2,1)}, u32[]{:S(2)}) copy-start(bf16[1,192,1536]{2,1,0:T(8,128)(2,1)} %param.8) | copy-start | bytes 1769476
  7.2 3.1 %copy-start.2 = (bf16[1,192,1536]{2,1,0:T(8,128)(2,1)S(1)}, bf16[1,192,1536]{2,1,0:T(8,128)(2,1)}, u32[]{:S(2)}) copy-start(bf16[1,192,1536]{2,1,0:T(8,128)(2,1)} %param.7) | copy-start | bytes 1769476
  7.2 124.5 %all-gather.6.cloned.1.call-start = ((), (), s32[]{:S(2)}) async-start(), calls=%async_computation.3 | async-start | bytes 5308416 | tf_op jit(solution)/shard_map/all_gather | solution.py:44
  22.8 80.7 %all-to-all-start = ((bf16[8,192,1,576]{3,1,2,0:T(8,128)(2,1)}), bf16[8,192,1,576]{3,1,2,0:T(8,128)(2,1)S(1)}, u32[]{:S(2)}, u32[]{:S(2)}) async-start(bf16[8,192,1,576]{3,1,2,0:T(8,128)(2,1)} %bitcast_dynamic-update-slice_fusion), calls=%async_computation | async-start | bytes 3932160 | tf_op jit(solution)/shard_map/all_to_all | solution.py:76
  28.1 127.9 %all-gather.4.cloned.1.call-start = ((), (), s32[]{:S(2)}) async-start(), calls=%async_computation.2 | async-start | bytes 4866048 | tf_op jit(solution)/shard_map/all_gather | solution.py:43
  34.3 29.6 %collective-permute-start = (bf16[192,384]{1,0:T(8,128)(2,1)}, bf16[192,384]{1,0:T(8,128)(2,1)}, u32[]{:S(2)}, u32[]{:S(2)}) collective-permute-start(bf16[192,384]{1,0:T(8,128)(2,1)} %bitcast.80), channel_id=1, source_target_pairs={{0,16},{2,18},{4,20},{6,22},{8,24},{10,26},{12,28},{14,30},{16,0},... | collective-permute-start | bytes 442376 | tf_op jit(solution)/shard_map/ppermute | solution.py:73
  37.3 30.1 %collective-permute-start.1 = (bf16[192,384]{1,0:T(8,128)(2,1)}, bf16[192,384]{1,0:T(8,128)(2,1)}, u32[]{:S(2)}, u32[]{:S(2)}) collective-permute-start(bf16[192,384]{1,0:T(8,128)(2,1)} %bitcast.79), channel_id=1, source_target_pairs={{0,18},{2,20},{4,22},{6,24},{8,26},{10,28},{12,30},{14,16},{16,2},... | collective-permute-start | bytes 442376 | tf_op jit(solution)/shard_map/ppermute | solution.py:73
  39.7 35.4 %collective-permute-start.2 = (bf16[192,384]{1,0:T(8,128)(2,1)}, bf16[192,384]{1,0:T(8,128)(2,1)}, u32[]{:S(2)}, u32[]{:S(2)}) collective-permute-start(bf16[192,384]{1,0:T(8,128)(2,1)} %bitcast.78), channel_id=1, source_target_pairs={{0,20},{2,22},{4,24},{6,26},{8,28},{10,30},{12,16},{14,18},{16,4},... | collective-permute-start | bytes 442376 | tf_op jit(solution)/shard_map/ppermute | solution.py:73
  42.7 35.7 %collective-permute-start.3 = (bf16[192,384]{1,0:T(8,128)(2,1)}, bf16[192,384]{1,0:T(8,128)(2,1)}, u32[]{:S(2)}, u32[]{:S(2)}) collective-permute-start(bf16[192,384]{1,0:T(8,128)(2,1)} %bitcast.77), channel_id=1, source_target_pairs={{0,22},{2,24},{4,26},{6,28},{8,30},{10,16},{12,18},{14,20},{16,6},... | collective-permute-start | bytes 442376 | tf_op jit(solution)/shard_map/ppermute | solution.py:73
  44.6 35.6 %collective-permute-start.4 = (bf16[192,384]{1,0:T(8,128)(2,1)}, bf16[192,384]{1,0:T(8,128)(2,1)}, u32[]{:S(2)}, u32[]{:S(2)}) collective-permute-start(bf16[192,384]{1,0:T(8,128)(2,1)} %bitcast.76), channel_id=1, source_target_pairs={{0,24},{2,26},{4,28},{6,30},{8,16},{10,18},{12,20},{14,22},{16,8},... | collective-permute-start | bytes 442376 | tf_op jit(solution)/shard_map/ppermute | solution.py:73
  63.9 32.9 %collective-permute-start.7 = (bf16[192,384]{1,0:T(8,128)(2,1)}, bf16[192,384]{1,0:T(8,128)(2,1)S(1)}, u32[]{:S(2)}, u32[]{:S(2)}) collective-permute-start(bf16[192,384]{1,0:T(8,128)(2,1)} %bitcast.73), channel_id=1, source_target_pairs={{0,30},{2,16},{4,18},{6,20},{8,22},{10,24},{12,26},{14,28},{16,14}... | collective-permute-start | bytes 442376 | tf_op jit(solution)/shard_map/ppermute | solution.py:73
  67.4 29.4 %collective-permute-start.5 = (bf16[192,384]{1,0:T(8,128)(2,1)S(1)}, bf16[192,384]{1,0:T(8,128)(2,1)S(1)}, u32[]{:S(2)}, u32[]{:S(2)}) collective-permute-start(bf16[192,384]{1,0:T(8,128)(2,1)S(1)} %bitcast.96), channel_id=1, source_target_pairs={{0,26},{2,28},{4,30},{6,16},{8,18},{10,20},{12,22},{14,24},{16,10}... | collective-permute-start | bytes 442376 | tf_op jit(solution)/shard_map/ppermute | solution.py:73
  75.1 28.4 %collective-permute-start.6 = (bf16[192,384]{1,0:T(8,128)(2,1)S(1)}, bf16[192,384]{1,0:T(8,128)(2,1)S(1)}, u32[]{:S(2)}, u32[]{:S(2)}) collective-permute-start(bf16[192,384]{1,0:T(8,128)(2,1)S(1)} %bitcast.95), channel_id=1, source_target_pairs={{0,28},{2,30},{4,16},{6,18},{8,20},{10,22},{12,24},{14,26},{16,12}... | collective-permute-start | bytes 442376 | tf_op jit(solution)/shard_map/ppermute | solution.py:73
  113.7 1.4 copy-start
  118.6 1.4 copy-start
  123.6 1.4 copy-start
  127.7 19.4 %all-to-all-start.1 = ((bf16[8,192,192]{2,1,0:T(8,128)(2,1)}), bf16[8,192,192]{2,1,0:T(8,128)(2,1)S(1)}, u32[]{:S(2)}, u32[]{:S(2)}) async-start(bf16[8,192,192]{2,1,0:T(8,128)(2,1)} %bitcast.4), calls=%async_computation.1 | async-start | bytes 1572864 | tf_op jit(solution)/shard_map/all_to_all | solution.py:47
  135.2 15.0 %collective-permute-start.8 = (f32[2,48,1536]{2,1,0:T(8,128)S(1)}, f32[2,48,1536]{2,1,0:T(8,128)}, u32[]{:S(2)}, u32[]{:S(2)}) collective-permute-start(f32[2,48,1536]{2,1,0:T(8,128)S(1)} %dynamic-slice_bitcast_fusion), channel_id=1, source_target_pairs={{0,1},{1,0},{2,3},{3,2},{4,5},{5,4},{6,7},{7,6},{8,9},{9,8},{10,11... | collective-permute-start | bytes 1769480 | tf_op jit(solution)/shard_map/ppermute | solution.py:102
  149.1 7.0 %copy-start.3 = (bf16[192,1536]{1,0:T(8,128)(2,1)S(1)}, bf16[192,1536]{1,0:T(8,128)(2,1)}, u32[]{:S(2)}) copy-start(bf16[192,1536]{1,0:T(8,128)(2,1)} %reshape.21) | copy-start | bytes 1769476
  151.4 9.0 %collective-permute-start.10 = (f32[48,1536]{1,0:T(8,128)S(1)}, f32[48,1536]{1,0:T(8,128)S(1)}, u32[]{:S(2)}, u32[]{:S(2)}) collective-permute-start(f32[48,1536]{1,0:T(8,128)S(1)} %get-tuple-element.78), channel_id=1, source_target_pairs={{0,2},{1,3},{2,6},{3,7},{4,10},{5,11},{6,14},{7,15},{8,18},{9,19},... | collective-permute-start | bytes 884744 | tf_op jit(solution)/shard_map/ppermute | solution.py:116
  152.5 15.9 %collective-permute-start.9 = (f32[48,1536]{1,0:T(8,128)S(1)}, f32[48,1536]{1,0:T(8,128)S(1)}, u32[]{:S(2)}, u32[]{:S(2)}) collective-permute-start(f32[48,1536]{1,0:T(8,128)S(1)} %get-tuple-element.79), channel_id=1, source_target_pairs={{0,0},{1,1},{2,4},{3,5},{4,8},{5,9},{6,12},{7,13},{8,16},{9,17},{1... | collective-permute-start | bytes 884744 | tf_op jit(solution)/shard_map/ppermute | solution.py:116
Sparse Core Ops, SparseCore 0:
  9.7 55.2 all-gather.5
  67.9 85.3 all-gather.3
